TPU v7x, 256 devices: a whole 4x4x8 slice. The times are simulated.
256 devices in a mesh: grp: 4 (over y), dom: 64 (over x, z, core).
Axes of the slice: x: 4, y: 4, z: 8, core: 2. Of those that a mesh axis runs over, the one named last changes fastest.
Arguments:
- right_side: float32 [16, 524288], P(None, ('grp', 'dom')), may hold values from -38 to 38
- tile_values: float32 [24576, 128, 128], P(('grp', 'dom')), may hold values from 0 to 1, as said below
- tile_rows: int32 [24576], P(('grp', 'dom')), may hold values from 0 to 15
- tile_cols: int32 [24576], P(('grp', 'dom')), may hold values from 0 to 63, as said below
- tile_count: int32 [256], P(('grp', 'dom')), may hold values from 24 to 96, as said below
Outputs:
- solution_field: float32 [16, 524288], P(None, ('grp', 'dom'))
- residual: float32 [16, 524288], P(None, ('grp', 'dom'))
Inputs may be any that keep to these rules, and one draw needn't show every extreme that they name: `tile_cols`: values w * 16 + j name block j of the device just below along dom (w = 0), of the device itself (w = 1), of the device just above along dom (w = 2), or of the device of the same dom index whose grp index differs in the lowest bit (w = 3). No slot of a device at the first dom index names w = 0, none at the last names w = 2. `tile_count`: some device has all 96 slots live. `tile_values`: each row of a tile has at least one nonzero entry.
All inputs are finite; a program needn't handle non-finite values.
Results may differ from a plain program's by a relative error of at most 0.0003.
Values sent between devices are 32-bit elements; how exact they have to be, the bound alone decides.
No kernel may reach another device: no remote copies, remote signals or barrier semaphores. Data moves between devices by JAX's collectives and lax.ppermute only.
A program may use at most 64 MiB of HBM per device.

v0:
```python
import jax
import jax.numpy as jnp
from jax import lax
from jax.sharding import PartitionSpec as P

TILE = 128
NBD = 16
ITERS = 3


batch_slots = 8
damping = 0.8


def with_halo(shard, sides, width):
    for axis, dim in sides:
        size, length = (lax.axis_size(axis), shard.shape[dim])
        up = [(i, (i + 1) % size) for i in range(size - 1)]
        down = [(j, i) for i, j in up]
        last = lax.slice_in_dim(shard, length - width, length, axis=dim)
        initial = lax.slice_in_dim(shard, 0, width, axis=dim)
        before = lax.ppermute(last, axis, up)
        after = lax.ppermute(initial, axis, down)
        shard = jnp.concatenate([before, shard, after], axis=dim)
    return shard


def partner_2(value, axis, stride):
    mask = 2**stride
    pairs = [(source, source ^ mask) for source in range(lax.axis_size(axis))]
    return lax.ppermute(value, axis, pairs)


def to_blocks(field):
    rows_here, points_here = field.shape
    return field.reshape(rows_here, points_here // TILE, TILE).transpose(1, 0, 2)


def from_blocks(blocks):
    return blocks.transpose(1, 0, 2).reshape(blocks.shape[1], blocks.shape[0] * blocks.shape[2])


def fetch_window(scaled):
    shard_width = scaled.shape[1]
    padded = with_halo(scaled, (("dom", 1),), shard_width)
    partner = partner_2(scaled, "grp", 0)
    return to_blocks(jnp.concatenate([padded, partner], axis=1))


def any_window(columns):
    return columns >= 0


def tile_pass(tiles, tile_rows, tile_cols, live_count, window_blocks, own_blocks, wanted):
    own_total = own_blocks.shape[0]
    window_total = window_blocks.shape[0]
    turns = (live_count + batch_slots - 1) // batch_slots

    def one_batch(turn, sums):
        row_sums, window_sums = sums
        first_slot = turn * batch_slots
        some_tiles = lax.dynamic_slice_in_dim(tiles, first_slot, batch_slots, 0)
        some_rows = lax.dynamic_slice_in_dim(tile_rows, first_slot, batch_slots, 0)
        some_cols = lax.dynamic_slice_in_dim(tile_cols, first_slot, batch_slots, 0)
        slot_ids = first_slot + jnp.arange(batch_slots, dtype=jnp.int32)
        active = ((slot_ids < live_count) & wanted(some_cols)).astype(jnp.float32)
        forward = jnp.einsum(
            "bij,bqj->bqi", some_tiles, window_blocks[some_cols], precision=lax.Precision.HIGHEST
        )
        backward = jnp.einsum(
            "bij,bqi->bqj", some_tiles, own_blocks[some_rows], precision=lax.Precision.HIGHEST
        )
        row_pick = (some_rows[:, None] == jnp.arange(own_total, dtype=jnp.int32)[None, :]).astype(
            jnp.float32
        ) * active[:, None]
        col_pick = (
            some_cols[:, None] == jnp.arange(window_total, dtype=jnp.int32)[None, :]
        ).astype(jnp.float32) * active[:, None]
        row_sums = row_sums + jnp.einsum(
            "bn,bqi->nqi", row_pick, forward, precision=lax.Precision.HIGHEST
        )
        window_sums = window_sums + jnp.einsum(
            "bn,bqi->nqi", col_pick, backward, precision=lax.Precision.HIGHEST
        )
        return (row_sums, window_sums)

    return lax.fori_loop(
        0, turns, one_batch, (jnp.zeros_like(own_blocks), jnp.zeros_like(window_blocks))
    )


def return_sums(row_sums, window_sums):
    shard_blocks = row_sums.shape[0]
    own_part = from_blocks(row_sums + window_sums[shard_blocks : 2 * shard_blocks])
    sideways = jnp.concatenate(
        [
            from_blocks(window_sums[:shard_blocks]),
            from_blocks(window_sums[2 * shard_blocks : 3 * shard_blocks]),
        ],
        axis=1,
    )
    shard_width = own_part.shape[1]
    returned = with_halo(sideways, (("dom", 1),), shard_width)
    across = partner_2(from_blocks(window_sums[3 * shard_blocks :]), "grp", 0)
    return own_part + returned[:, :shard_width] + returned[:, 3 * shard_width :] + across


def degrees(tiles, tile_rows, tile_cols, live_count):
    slot_total = tiles.shape[0]
    active = (jnp.arange(slot_total, dtype=jnp.int32) < live_count).astype(jnp.float32)
    row_pick = (tile_rows[:, None] == jnp.arange(NBD, dtype=jnp.int32)[None, :]).astype(
        jnp.float32
    ) * active[:, None]
    col_pick = (tile_cols[:, None] == jnp.arange(4 * NBD, dtype=jnp.int32)[None, :]).astype(
        jnp.float32
    ) * active[:, None]
    row_sums = jnp.einsum(
        "tn,ti->ni", row_pick, jnp.sum(tiles, axis=2), precision=lax.Precision.HIGHEST
    )[:, None, :]
    window_sums = jnp.einsum(
        "tn,ti->ni", col_pick, jnp.sum(tiles, axis=1), precision=lax.Precision.HIGHEST
    )[:, None, :]
    return 1.0 + return_sums(row_sums, window_sums)[0]


def apply_operator(field, point_scale, tiles, tile_rows, tile_cols, live_count):
    scaled = point_scale * field
    own_blocks = to_blocks(scaled)
    row_sums, window_sums = tile_pass(
        tiles, tile_rows, tile_cols, live_count, fetch_window(scaled), own_blocks, any_window
    )
    return field - damping * point_scale * return_sums(row_sums, window_sums)


def squares(residual):
    return lax.psum(jnp.sum(residual * residual, axis=1), ("grp", "dom"))


def per_device(right_side, tile_values, tile_rows, tile_cols, tile_count):
    live_count = tile_count[0]
    point_scale = 1.0 / jnp.sqrt(degrees(tile_values, tile_rows, tile_cols, live_count))
    solution_field = jnp.zeros_like(right_side)
    residual = right_side
    direction = right_side
    norm_now = squares(residual)
    for iteration in range(ITERS):
        image = apply_operator(
            direction, point_scale, tile_values, tile_rows, tile_cols, live_count
        )
        curvature = lax.psum(jnp.sum(direction * image, axis=1), ("grp", "dom"))
        step_size = norm_now / curvature
        solution_field = solution_field + step_size[:, None] * direction
        residual = residual - step_size[:, None] * image
        norm_next = squares(residual)
        direction = residual + (norm_next / norm_now)[:, None] * direction
        norm_now = norm_next
    return (solution_field, residual)


def solution(mesh):
    placed = (
        P(None, ("grp", "dom")),
        P(("grp", "dom"), None, None),
        P(("grp", "dom")),
        P(("grp", "dom")),
        P(("grp", "dom")),
    )
    return jax.shard_map(
        per_device,
        mesh=mesh,
        in_specs=placed,
        out_specs=(P(None, ("grp", "dom")), P(None, ("grp", "dom"))),
        check_vma=False,
    )
```

profile of v0, /device:TPU:8, one launch (start us, length us, event | category | flops | bytes accessed | tf_op | source)
XLA Modules:
  0.0 699.6 jit_solution(14309244955130155435)
XLA Ops:
  0.7 4.5 fusion.83
  6.2 2.2 collective-permute-start.2
  9.7 3.0 collective-permute-start
  15.0 3.6 collective-permute-start.3
  19.7 80.8 %while.36 = (s32[]{:T(128)}, f32[16,16,128]{2,0,1:T(8,128)S(1)}, f32[64,16,128]{2,0,1:T(8,128)S(1)}, s32[]{:T(128)}, s32[96]{0:T(128)S(1)}, /*index=5*/s32[]{:T(...) while((s32[]{:T(128)}, f32[16,16,128]{2,0,1:T(8,128)S(1)}, ...), condition=%wide.region_5.6_spmd, body=%wide.region_4.5_spmd.sunk | while | flops 66227548 | bytes 3023571 | solution.py:87
  21.0 2.0 fusion.138
  27.8 2.0 fusion.138
  34.5 2.0 fusion.138
  41.3 2.0 fusion.138
  48.0 2.0 fusion.138
  54.7 2.0 fusion.138
  61.5 2.0 fusion.138
  102.2 3.0 collective-permute-start.6
  106.4 91.1 %all-reduce = (f32[16]{0:T(128)S(1)}, f32[16]{0:T(128)S(1)}) all-reduce(f32[16]{0:T(128)S(1)} %get-tuple-element.173, f32[16]{0:T(128)S(1)} %get-tuple-element.172), channel_id=1, replica_groups=mesh['grp'=4,'dom'=64] {'grp','dom'}, use_global_device_ids=true, to_apply=%region_1.0 | all-reduce | flops 32 | bytes 256 | tf_op jit(solution)/shard_map/psum | solution.py:136
  197.7 74.2 %psum.44 = f32[16]{0:T(128)S(1)} all-reduce(f32[16]{0:T(128)S(1)} %multiply_reduce_fusion.3), channel_id=1, replica_groups=mesh['grp'=4,'dom'=64] {'grp','dom'}, use_global_device_ids=true, to_apply=%region_9.10 | all-reduce | flops 16 | bytes 128 | tf_op jit(solution)/shard_map/psum | solution.py:136
  274.4 3.0 collective-permute-start.9
  278.5 80.8 %while.37 = (s32[]{:T(128)}, f32[16,16,128]{2,0,1:T(8,128)S(1)}, f32[64,16,128]{2,0,1:T(8,128)S(1)}, s32[]{:T(128)}, s32[96]{0:T(128)S(1)}, /*index=5*/s32[]{:T(...) while((s32[]{:T(128)}, f32[16,16,128]{2,0,1:T(8,128)S(1)}, ...), condition=%wide.region_11.12_spmd, body=%wide.region_10.11_spmd.sunk | while | flops 66227548 | bytes 3023571 | solution.py:87
  361.0 3.0 collective-permute-start.12
  365.2 83.0 %psum.45 = f32[16]{0:T(128)S(1)} all-reduce(f32[16]{0:T(128)S(1)} %get-tuple-element.254), channel_id=1, replica_groups=mesh['grp'=4,'dom'=64] {'grp','dom'}, use_global_device_ids=true, to_apply=%region_13.14 | all-reduce | flops 16 | bytes 128 | tf_op jit(solution)/shard_map/psum | solution.py:150
  448.4 74.2 %psum.46 = f32[16]{0:T(128)S(1)} all-reduce(f32[16]{0:T(128)S(1)} %get-tuple-element.252), channel_id=1, replica_groups=mesh['grp'=4,'dom'=64] {'grp','dom'}, use_global_device_ids=true, to_apply=%region_15.16 | all-reduce | flops 16 | bytes 128 | tf_op jit(solution)/shard_map/psum | solution.py:136
  525.1 3.0 collective-permute-start.15
  529.2 80.8 %while.38 = (s32[]{:T(128)}, f32[16,16,128]{2,0,1:T(8,128)S(1)}, f32[64,16,128]{2,0,1:T(8,128)S(1)}, s32[]{:T(128)}, s32[96]{0:T(128)S(1)}, /*index=5*/s32[]{:T(...) while((s32[]{:T(128)}, f32[16,16,128]{2,0,1:T(8,128)S(1)}, ...), condition=%wide.region_17.18_spmd, body=%wide.region_16.17_spmd.sunk | while | flops 66227548 | bytes 3023571 | solution.py:87
  611.7 3.0 collective-permute-start.18
  615.9 82.9 %psum.47 = f32[16]{0:T(128)S(1)} all-reduce(f32[16]{0:T(128)S(1)} %get-tuple-element.248), channel_id=1, replica_groups=mesh['grp'=4,'dom'=64] {'grp','dom'}, use_global_device_ids=true, to_apply=%region_19.20 | all-reduce | flops 16 | bytes 128 | tf_op jit(solution)/shard_map/psum | solution.py:150
  (472 shorter events, 247.9 us)
Async XLA Ops:
  0.6 5.2 copy-start.1
  0.6 12.1 %copy-start.2 = (s32[96]{0:T(128)S(1)}, s32[96]{0:T(128)}, u32[]{:S(2)}) copy-start(s32[96]{0:T(128)} %param.13) | copy-start | bytes 1156
  0.6 13.0 %copy-start = (f32[16,2048]{1,0:T(8,128)S(1)}, f32[16,2048]{1,0:T(8,128)}, u32[]{:S(2)}) copy-start(f32[16,2048]{1,0:T(8,128)} %param.11) | copy-start | bytes 393220
  6.2 6.9 collective-permute-start.2
  8.4 4.7 collective-permute-start.1
  9.7 3.8 collective-permute-start
  13.6 5.8 collective-permute-start.5
  13.8 5.7 collective-permute-start.4
  15.0 4.6 collective-permute-start.3
  100.7 5.1 collective-permute-start.8
  100.8 4.9 collective-permute-start.7
  102.2 4.0 collective-permute-start.6
  272.0 5.5 collective-permute-start.11
  273.1 4.4 collective-permute-start.10
  274.4 4.0 collective-permute-start.9
  359.5 5.1 collective-permute-start.14
  359.6 4.9 collective-permute-start.13
  361.0 4.0 collective-permute-start.12
  522.7 5.5 collective-permute-start.17
  523.8 4.4 collective-permute-start.16
  525.1 4.0 collective-permute-start.15
  610.2 5.1 collective-permute-start.20
  610.3 4.9 collective-permute-start.19
  611.7 4.0 collective-permute-start.18
where the time goes:
time: 706 us; the launch traced here: 700 us
  blocking collectives  405 us (57%)
  matrix products  171 us (24%)
  local copies, waits for them, and re-layouts  40.5 us (6%)
  other arithmetic  36.7 us (5%)
  starting transfers between devices  35.7 us (5%)
    psum x3, blocking collectives, squares(): return lax.psum(jnp.sum(residual * residual, axis=1), ('grp', 'dom'))  240 us
    psum x2, blocking collectives, per_device(): curvature = lax.psum(jnp.sum(direction * image, axis=1), ('grp', 'dom'))  166 us
    dot_general x36, matrix products, one_batch(): jnp.einsum('bij,bqj->bqi', some_tiles, window_blocks[some_cols], precisio...  70.4 us
    dot_general x36, matrix products, one_batch(): jnp.einsum('bij,bqi->bqj', some_tiles, own_blocks[some_rows], precision=l...  56.9 us
    dot_general x36, matrix products, one_batch(): jnp.einsum('bn,bqi->nqi', col_pick, backward, precision=lax.Precision.HIG...  28.6 us
    convert_element_type x36, other arithmetic, one_batch(): active = ((slot_ids < live_count) & wanted(some_cols)).astype(jnp.float32)  26.1 us
    ppermute x7, starting transfers between devices, with_halo(): before = lax.ppermute(last, axis, up)  21.8 us
    gather x36, local copies, waits for them, and re-layouts, one_batch(): own_blocks[some_rows]  20 us
  transfers between devices with their start and end apart: 21, of which 11 were waited for; matrix products, arithmetic and copies ran while one was open for 0% of the time, Pallas kernels for 0%

commit v1 on v0

--- a/solution.py
+++ b/solution.py
@@ -54,39 +54,24 @@
 def tile_pass(tiles, tile_rows, tile_cols, live_count, window_blocks, own_blocks, wanted):
     own_total = own_blocks.shape[0]
     window_total = window_blocks.shape[0]
-    turns = (live_count + batch_slots - 1) // batch_slots
-
-    def one_batch(turn, sums):
-        row_sums, window_sums = sums
-        first_slot = turn * batch_slots
-        some_tiles = lax.dynamic_slice_in_dim(tiles, first_slot, batch_slots, 0)
-        some_rows = lax.dynamic_slice_in_dim(tile_rows, first_slot, batch_slots, 0)
-        some_cols = lax.dynamic_slice_in_dim(tile_cols, first_slot, batch_slots, 0)
-        slot_ids = first_slot + jnp.arange(batch_slots, dtype=jnp.int32)
-        active = ((slot_ids < live_count) & wanted(some_cols)).astype(jnp.float32)
-        forward = jnp.einsum(
-            "bij,bqj->bqi", some_tiles, window_blocks[some_cols], precision=lax.Precision.HIGHEST
-        )
-        backward = jnp.einsum(
-            "bij,bqi->bqj", some_tiles, own_blocks[some_rows], precision=lax.Precision.HIGHEST
-        )
-        row_pick = (some_rows[:, None] == jnp.arange(own_total, dtype=jnp.int32)[None, :]).astype(
-            jnp.float32
-        ) * active[:, None]
-        col_pick = (
-            some_cols[:, None] == jnp.arange(window_total, dtype=jnp.int32)[None, :]
-        ).astype(jnp.float32) * active[:, None]
-        row_sums = row_sums + jnp.einsum(
-            "bn,bqi->nqi", row_pick, forward, precision=lax.Precision.HIGHEST
-        )
-        window_sums = window_sums + jnp.einsum(
-            "bn,bqi->nqi", col_pick, backward, precision=lax.Precision.HIGHEST
-        )
-        return (row_sums, window_sums)
-
-    return lax.fori_loop(
-        0, turns, one_batch, (jnp.zeros_like(own_blocks), jnp.zeros_like(window_blocks))
+    slot_total = tiles.shape[0]
+    slot_ids = jnp.arange(slot_total, dtype=jnp.int32)
+    active = ((slot_ids < live_count) & wanted(tile_cols)).astype(jnp.float32)
+    forward = jnp.einsum(
+        "bij,bqj->bqi", tiles, window_blocks[tile_cols], precision=lax.Precision.HIGHEST
     )
+    backward = jnp.einsum(
+        "bij,bqi->bqj", tiles, own_blocks[tile_rows], precision=lax.Precision.HIGHEST
+    )
+    row_pick = (tile_rows[:, None] == jnp.arange(own_total, dtype=jnp.int32)[None, :]).astype(
+        jnp.float32
+    ) * active[:, None]
+    col_pick = (tile_cols[:, None] == jnp.arange(window_total, dtype=jnp.int32)[None, :]).astype(
+        jnp.float32
+    ) * active[:, None]
+    row_sums = jnp.einsum("bn,bqi->nqi", row_pick, forward, precision=lax.Precision.HIGHEST)
+    window_sums = jnp.einsum("bn,bqi->nqi", col_pick, backward, precision=lax.Precision.HIGHEST)
+    return (row_sums, window_sums)
 
 
 def return_sums(row_sums, window_sums):

time: 706 us -> 521 us (0.74)
  matrix products: 171 us -> 62.4 us
  local copies, waits for them, and re-layouts: 40.5 us -> 4.97 us
  other arithmetic: 36.7 us -> 7.95 us
  blocking collectives: 405 us -> 391 us
    dot_general x144 -> x12, matrix products: 170 us -> 62.1 us  [the longest x3 35.5 us: tile_pass(): jnp.einsum('bij,bqj->bqi', tiles, window_blocks[tile_cols], precision=lax...]
    gather x72 -> x6, local copies, waits for them, and re-layouts: 39.9 us -> 4.39 us  [the longest x3 2.2 us: tile_pass(): own_blocks[tile_rows]]
    convert_element_type x37 -> x1, other arithmetic: 26.1 us -> 0.01 us  [tile_pass(): active = ((slot_ids < live_count) & wanted(tile_cols)).astype(jnp.float32)]
    psum x3, blocking collectives: 240 us -> 232 us  [squares(): return lax.psum(jnp.sum(residual * residual, axis=1), ('grp', 'dom'))]
  transfers between devices with their start and end apart: 21 -> 21, of which waited for: 11 -> 1; matrix products, arithmetic and copies ran while one was open for 0% -> 13% of each run, Pallas kernels for 0% -> 0%
where the time goes in v1:
time: 521 us; the launch traced here: 513 us
  blocking collectives  391 us (75%)
  matrix products  62.4 us (12%)
  starting transfers between devices  42.3 us (8%)
  other arithmetic  7.95 us (2%)
    psum x3, blocking collectives, squares(): return lax.psum(jnp.sum(residual * residual, axis=1), ('grp', 'dom'))  232 us
    psum x2, blocking collectives, per_device(): curvature = lax.psum(jnp.sum(direction * image, axis=1), ('grp', 'dom'))  159 us
    dot_general x3, matrix products, tile_pass(): jnp.einsum('bij,bqj->bqi', tiles, window_blocks[tile_cols], precision=lax...  35.5 us
    ppermute x7, starting transfers between devices, with_halo(): before = lax.ppermute(last, axis, up)  24.5 us
    dot_general x3, matrix products, tile_pass(): jnp.einsum('bij,bqi->bqj', tiles, own_blocks[tile_rows], precision=lax.Pr...  22.1 us
  transfers between devices with their start and end apart: 21, of which 1 were waited for; matrix products, arithmetic and copies ran while one was open for 13% of the time, Pallas kernels for 0%

profile of v1, /device:TPU:8, one launch (start us, length us, event | category | flops | bytes accessed | tf_op | source)
XLA Modules:
  0.0 513.1 jit_solution(16996441749000243244)
XLA Ops:
  1.3 4.5 fusion.68
  6.1 2.2 collective-permute-start.2
  9.6 1.3 collective-permute-start.1
  11.1 1.9 collective-permute-done.1
  13.2 1.7 collective-permute-start.5
  16.1 4.7 collective-permute-start.3
  21.5 7.4 %fusion.77 = f32[96,16,128]{2,1,0:T(8,128)S(1)} fusion(f32[96,16,128]{2,1,0:T(8,128)S(1)} %gather_fusion.1, f32[96,128,128]{2,1,0:T(8,128)} %param.6), kind=kOutput, calls=%fused_computation.130 | convolution fusion | flops 301989888 | bytes 7864320 | tf_op jit(solution)/shard_map/bij,bqi->bqj/dot_general | solution.py:63
  31.7 4.2 collective-permute-start.6
  36.7 11.8 %fusion.76 = f32[96,16,128]{2,1,0:T(8,128)S(1)} fusion(f32[96,16,128]{2,1,0:T(8,128)S(1)} %gather_fusion, f32[96,128,128]{2,1,0:T(8,128)} %param.6), kind=kOutput, calls=%fused_computation.129 | convolution fusion | flops 301989888 | bytes 7864320 | tf_op jit(solution)/shard_map/bij,bqj->bqi/dot_general | solution.py:60
  49.4 84.8 %all-reduce = (f32[16]{0:T(128)S(1)}, f32[16]{0:T(128)S(1)}) all-reduce(f32[16]{0:T(128)S(1)} %get-tuple-element.5, f32[16]{0:T(128)S(1)} %get-tuple-element.4), channel_id=1, replica_groups=mesh['grp'=4,'dom'=64] {'grp','dom'}, use_global_device_ids=true, to_apply=%region_1.0 | all-reduce | flops 32 | bytes 256 | tf_op jit(solution)/shard_map/psum | solution.py:121
  134.5 73.4 %psum.44 = f32[16]{0:T(128)S(1)} all-reduce(f32[16]{0:T(128)S(1)} %multiply_reduce_fusion.3), channel_id=1, replica_groups=mesh['grp'=4,'dom'=64] {'grp','dom'}, use_global_device_ids=true, to_apply=%region_7.0 | all-reduce | flops 16 | bytes 128 | tf_op jit(solution)/shard_map/psum | solution.py:121
  210.3 3.0 collective-permute-start.9
  214.1 7.4 %fusion.79 = f32[96,16,128]{2,1,0:T(8,128)S(1)} fusion(f32[96,16,128]{2,1,0:T(8,128)S(1)} %gather_fusion.3, f32[96,128,128]{2,1,0:T(8,128)} %param.6), kind=kOutput, calls=%fused_computation.132 | convolution fusion | flops 301989888 | bytes 7864320 | tf_op jit(solution)/shard_map/bij,bqi->bqj/dot_general | solution.py:63
  224.9 4.1 collective-permute-start.12
  229.9 11.8 %fusion.78 = f32[96,16,128]{2,1,0:T(8,128)S(1)} fusion(f32[96,16,128]{2,1,0:T(8,128)S(1)} %gather_fusion.2, f32[96,128,128]{2,1,0:T(8,128)} %param.6), kind=kOutput, calls=%fused_computation.131 | convolution fusion | flops 301989888 | bytes 7864320 | tf_op jit(solution)/shard_map/bij,bqj->bqi/dot_general | solution.py:60
  242.6 79.7 %psum.45 = f32[16]{0:T(128)S(1)} all-reduce(f32[16]{0:T(128)S(1)} %get-tuple-element.14), channel_id=1, replica_groups=mesh['grp'=4,'dom'=64] {'grp','dom'}, use_global_device_ids=true, to_apply=%region_9.0 | all-reduce | flops 16 | bytes 128 | tf_op jit(solution)/shard_map/psum | solution.py:135
  322.5 73.3 %psum.46 = f32[16]{0:T(128)S(1)} all-reduce(f32[16]{0:T(128)S(1)} %get-tuple-element.12), channel_id=1, replica_groups=mesh['grp'=4,'dom'=64] {'grp','dom'}, use_global_device_ids=true, to_apply=%region_11.0 | all-reduce | flops 16 | bytes 128 | tf_op jit(solution)/shard_map/psum | solution.py:121
  398.1 3.0 collective-permute-start.15
  401.9 7.4 %fusion.81 = f32[96,16,128]{2,1,0:T(8,128)S(1)} fusion(f32[96,16,128]{2,1,0:T(8,128)S(1)} %gather_fusion.5, f32[96,128,128]{2,1,0:T(8,128)} %param.6), kind=kOutput, calls=%fused_computation.134 | convolution fusion | flops 301989888 | bytes 7864320 | tf_op jit(solution)/shard_map/bij,bqi->bqj/dot_general | solution.py:63
  411.7 1.4 collective-permute-start.20
  413.0 4.2 collective-permute-start.18
  418.1 11.8 %fusion.80 = f32[96,16,128]{2,1,0:T(8,128)S(1)} fusion(f32[96,16,128]{2,1,0:T(8,128)S(1)} %gather_fusion.4, f32[96,128,128]{2,1,0:T(8,128)} %param.6), kind=kOutput, calls=%fused_computation.133 | convolution fusion | flops 301989888 | bytes 7864320 | tf_op jit(solution)/shard_map/bij,bqj->bqi/dot_general | solution.py:60
  430.9 79.7 %psum.47 = f32[16]{0:T(128)S(1)} all-reduce(f32[16]{0:T(128)S(1)} %get-tuple-element.8), channel_id=1, replica_groups=mesh['grp'=4,'dom'=64] {'grp','dom'}, use_global_device_ids=true, to_apply=%region_13.0 | all-reduce | flops 16 | bytes 128 | tf_op jit(solution)/shard_map/psum | solution.py:135
  511.2 1.5 multiply_subtract_fusion
  (111 shorter events, 24.5 us)
Async XLA Ops:
  5.9 235.8 %copy-start.1 = (f32[96]{0:T(128)}, f32[96]{0:T(128)S(1)}, u32[]{:S(2)}) copy-start(f32[96]{0:T(128)S(1)} %get-tuple-element.35) | copy-start | bytes 1156
  6.1 5.1 collective-permute-start.2
  8.3 2.8 collective-permute-start
  9.6 3.5 collective-permute-start.1
  10.9 218.2 %copy-start.9 = (s32[1024]{0:T(1024)}, s32[1024]{0:T(1024)S(1)}, u32[]{:S(2)}) copy-start(s32[1024]{0:T(1024)S(1)} %pad_clamp_fusion.1) | copy-start | bytes 12292
  13.2 18.5 %collective-permute-start.5 = (f32[16,2048]{1,0:T(8,128)S(1)}, f32[16,2048]{1,0:T(8,128)S(1)}, u32[]{:S(2)}, u32[]{:S(2)}) collective-permute-start(f32[16,2048]{1,0:T(8,128)S(1)} %broadcast_multiply_fusion.2), channel_id=1, source_target_pairs={{0,64},{64,0},{128,192},{192,128},{1,65},{65,1},{129,193},{193,129... | collective-permute-start | bytes 393224 | tf_op jit(solution)/shard_map/ppermute | solution.py:31
  14.8 21.0 %collective-permute-start.4 = (f32[16,2048]{1,0:T(8,128)S(1)}, f32[16,2048]{1,0:T(8,128)S(1)}, u32[]{:S(2)}, u32[]{:S(2)}) collective-permute-start(f32[16,2048]{1,0:T(8,128)S(1)} %broadcast_multiply_fusion.2), channel_id=1, source_target_pairs={{1,0},{2,1},{3,2},{4,3},{5,4},{6,5},{7,6},{8,7},{9,8},{10,9},{11,1... | collective-permute-start | bytes 393224 | tf_op jit(solution)/shard_map/ppermute | solution.py:23
  16.1 19.8 %collective-permute-start.3 = (f32[16,2048]{1,0:T(8,128)S(1)}, f32[16,2048]{1,0:T(8,128)S(1)}, u32[]{:S(2)}, u32[]{:S(2)}) collective-permute-start(f32[16,2048]{1,0:T(8,128)S(1)} %broadcast_multiply_fusion.2), channel_id=1, source_target_pairs={{0,1},{1,2},{2,3},{3,4},{4,5},{5,6},{6,7},{7,8},{8,9},{9,10},{10,1... | collective-permute-start | bytes 393224 | tf_op jit(solution)/shard_map/ppermute | solution.py:22
  29.9 19.3 %collective-permute-start.7 = (f32[16,2048]{1,0:T(8,128)S(1)}, f32[16,2048]{1,0:T(8,128)S(1)}, u32[]{:S(2)}, u32[]{:S(2)}) collective-permute-start(f32[16,2048]{1,0:T(8,128)S(1)} %bitcast.188), channel_id=1, source_target_pairs={{1,0},{2,1},{3,2},{4,3},{5,4},{6,5},{7,6},{8,7},{9,8},{10,9},{11,1... | collective-permute-start | bytes 393224 | tf_op jit(solution)/shard_map/ppermute | solution.py:23
  31.2 18.0 %collective-permute-start.8 = (f32[16,2048]{1,0:T(8,128)S(1)}, f32[16,2048]{1,0:T(8,128)S(1)}, u32[]{:S(2)}, u32[]{:S(2)}) collective-permute-start(f32[16,2048]{1,0:T(8,128)S(1)} %bitcast.185), channel_id=1, source_target_pairs={{0,64},{64,0},{128,192},{192,128},{1,65},{65,1},{129,193},{193,129... | collective-permute-start | bytes 393224 | tf_op jit(solution)/shard_map/ppermute | solution.py:31
  31.7 17.5 %collective-permute-start.6 = (f32[16,2048]{1,0:T(8,128)S(1)}, f32[16,2048]{1,0:T(8,128)S(1)}, u32[]{:S(2)}, u32[]{:S(2)}) collective-permute-start(f32[16,2048]{1,0:T(8,128)S(1)} %bitcast.182), channel_id=1, source_target_pairs={{0,1},{1,2},{2,3},{3,4},{4,5},{5,6},{6,7},{7,8},{8,9},{9,10},{10,1... | collective-permute-start | bytes 393224 | tf_op jit(solution)/shard_map/ppermute | solution.py:22
  134.3 262.5 %copy-start.8 = (f32[16]{0:T(128)}, f32[16]{0:T(128)S(1)}, u32[]{:S(2)}) copy-start(f32[16]{0:T(128)S(1)} %div.16) | copy-start | bytes 196
  208.0 16.9 %collective-permute-start.11 = (f32[16,2048]{1,0:T(8,128)S(1)}, f32[16,2048]{1,0:T(8,128)S(1)}, u32[]{:S(2)}, u32[]{:S(2)}) collective-permute-start(f32[16,2048]{1,0:T(8,128)S(1)} %get-tuple-element.16), channel_id=1, source_target_pairs={{0,64},{64,0},{128,192},{192,128},{1,65},{65,1},{129,193},{193,129... | collective-permute-start | bytes 393224 | tf_op jit(solution)/shard_map/ppermute | solution.py:31
  209.1 20.0 %collective-permute-start.10 = (f32[16,2048]{1,0:T(8,128)S(1)}, f32[16,2048]{1,0:T(8,128)S(1)}, u32[]{:S(2)}, u32[]{:S(2)}) collective-permute-start(f32[16,2048]{1,0:T(8,128)S(1)} %get-tuple-element.16), channel_id=1, source_target_pairs={{1,0},{2,1},{3,2},{4,3},{5,4},{6,5},{7,6},{8,7},{9,8},{10,9},{11,1... | collective-permute-start | bytes 393224 | tf_op jit(solution)/shard_map/ppermute | solution.py:23
  210.3 18.7 %collective-permute-start.9 = (f32[16,2048]{1,0:T(8,128)S(1)}, f32[16,2048]{1,0:T(8,128)S(1)}, u32[]{:S(2)}, u32[]{:S(2)}) collective-permute-start(f32[16,2048]{1,0:T(8,128)S(1)} %get-tuple-element.16), channel_id=1, source_target_pairs={{0,1},{1,2},{2,3},{3,4},{4,5},{5,6},{6,7},{7,8},{8,9},{9,10},{10,1... | collective-permute-start | bytes 393224 | tf_op jit(solution)/shard_map/ppermute | solution.py:22
  222.5 19.9 %collective-permute-start.13 = (f32[16,2048]{1,0:T(8,128)S(1)}, f32[16,2048]{1,0:T(8,128)S(1)}, u32[]{:S(2)}, u32[]{:S(2)}) collective-permute-start(f32[16,2048]{1,0:T(8,128)S(1)} %bitcast.189), channel_id=1, source_target_pairs={{1,0},{2,1},{3,2},{4,3},{5,4},{6,5},{7,6},{8,7},{9,8},{10,9},{11,1... | collective-permute-start | bytes 393224 | tf_op jit(solution)/shard_map/ppermute | solution.py:23
  223.8 18.6 %collective-permute-start.14 = (f32[16,2048]{1,0:T(8,128)S(1)}, f32[16,2048]{1,0:T(8,128)S(1)}, u32[]{:S(2)}, u32[]{:S(2)}) collective-permute-start(f32[16,2048]{1,0:T(8,128)S(1)} %bitcast.186), channel_id=1, source_target_pairs={{0,64},{64,0},{128,192},{192,128},{1,65},{65,1},{129,193},{193,129... | collective-permute-start | bytes 393224 | tf_op jit(solution)/shard_map/ppermute | solution.py:31
  224.9 17.5 %collective-permute-start.12 = (f32[16,2048]{1,0:T(8,128)S(1)}, f32[16,2048]{1,0:T(8,128)S(1)}, u32[]{:S(2)}, u32[]{:S(2)}) collective-permute-start(f32[16,2048]{1,0:T(8,128)S(1)} %bitcast.183), channel_id=1, source_target_pairs={{0,1},{1,2},{2,3},{3,4},{4,5},{5,6},{6,7},{7,8},{8,9},{9,10},{10,1... | collective-permute-start | bytes 393224 | tf_op jit(solution)/shard_map/ppermute | solution.py:22
  395.9 17.1 %collective-permute-start.17 = (f32[16,2048]{1,0:T(8,128)S(1)}, f32[16,2048]{1,0:T(8,128)S(1)}, u32[]{:S(2)}, u32[]{:S(2)}) collective-permute-start(f32[16,2048]{1,0:T(8,128)S(1)} %get-tuple-element.10), channel_id=1, source_target_pairs={{0,64},{64,0},{128,192},{192,128},{1,65},{65,1},{129,193},{193,129... | collective-permute-start | bytes 393224 | tf_op jit(solution)/shard_map/ppermute | solution.py:31
  396.8 20.4 %collective-permute-start.16 = (f32[16,2048]{1,0:T(8,128)S(1)}, f32[16,2048]{1,0:T(8,128)S(1)}, u32[]{:S(2)}, u32[]{:S(2)}) collective-permute-start(f32[16,2048]{1,0:T(8,128)S(1)} %get-tuple-element.10), channel_id=1, source_target_pairs={{1,0},{2,1},{3,2},{4,3},{5,4},{6,5},{7,6},{8,7},{9,8},{10,9},{11,1... | collective-permute-start | bytes 393224 | tf_op jit(solution)/shard_map/ppermute | solution.py:23
  398.1 19.1 %collective-permute-start.15 = (f32[16,2048]{1,0:T(8,128)S(1)}, f32[16,2048]{1,0:T(8,128)S(1)}, u32[]{:S(2)}, u32[]{:S(2)}) collective-permute-start(f32[16,2048]{1,0:T(8,128)S(1)} %get-tuple-element.10), channel_id=1, source_target_pairs={{0,1},{1,2},{2,3},{3,4},{4,5},{5,6},{6,7},{7,8},{8,9},{9,10},{10,1... | collective-permute-start | bytes 393224 | tf_op jit(solution)/shard_map/ppermute | solution.py:22
  410.4 20.3 %collective-permute-start.19 = (f32[16,2048]{1,0:T(8,128)S(1)}, f32[16,2048]{1,0:T(8,128)S(1)}, u32[]{:S(2)}, u32[]{:S(2)}) collective-permute-start(f32[16,2048]{1,0:T(8,128)S(1)} %bitcast.187), channel_id=1, source_target_pairs={{1,0},{2,1},{3,2},{4,3},{5,4},{6,5},{7,6},{8,7},{9,8},{10,9},{11,1... | collective-permute-start | bytes 393224 | tf_op jit(solution)/shard_map/ppermute | solution.py:23
  411.7 19.0 %collective-permute-start.20 = (f32[16,2048]{1,0:T(8,128)S(1)}, f32[16,2048]{1,0:T(8,128)S(1)}, u32[]{:S(2)}, u32[]{:S(2)}) collective-permute-start(f32[16,2048]{1,0:T(8,128)S(1)} %bitcast.184), channel_id=1, source_target_pairs={{0,64},{64,0},{128,192},{192,128},{1,65},{65,1},{129,193},{193,129... | collective-permute-start | bytes 393224 | tf_op jit(solution)/shard_map/ppermute | solution.py:31
  413.0 17.6 %collective-permute-start.18 = (f32[16,2048]{1,0:T(8,128)S(1)}, f32[16,2048]{1,0:T(8,128)S(1)}, u32[]{:S(2)}, u32[]{:S(2)}) collective-permute-start(f32[16,2048]{1,0:T(8,128)S(1)} %bitcast.181), channel_id=1, source_target_pairs={{0,1},{1,2},{2,3},{3,4},{4,5},{5,6},{6,7},{7,8},{8,9},{9,10},{10,1... | collective-permute-start | bytes 393224 | tf_op jit(solution)/shard_map/ppermute | solution.py:22
  (11 other events, 790.0 us)
